TPU v7x, 512 devices: a whole 4x8x8 slice. The times are simulated.
512 devices in a mesh: seq: 16 (over z, core), mlp: 8 (over y), tp: 4 (over x).
Axes of the slice: x: 4, y: 8, z: 8, core: 2. Of those that a mesh axis runs over, the one named last changes fastest.
Arguments:
- hidden: bfloat16 [64, 2048], P('mlp'), may hold values from -6 to 6
- lengths: int32 [64], P('mlp'), may hold values from 4 to 8192, as said below
- attention_gain: bfloat16 [2048], replicated, may hold values from 0.099609375 to 1.8984375
- query_weight: bfloat16 [2048, 2048], P('seq', 'tp'), may hold values from -0.125 to 0.125
- key_weight: bfloat16 [2048, 512], P('seq', 'tp'), may hold values from -0.125 to 0.125
- value_weight: bfloat16 [2048, 512], P('seq', 'tp'), may hold values from -0.125 to 0.125
- cached_keys: bfloat16 [64, 8192, 512], P('mlp', 'seq', 'tp'), may hold values from -800 to 800
- cached_values: bfloat16 [64, 8192, 512], P('mlp', 'seq', 'tp'), may hold values from -8 to 8
- output_weight: bfloat16 [2048, 2048], P('tp', 'seq'), may hold values from -0.125 to 0.125
- feedforward_gain: bfloat16 [2048], replicated, may hold values from 0.099609375 to 1.8984375
- gate_weight: bfloat16 [2048, 8192], P('mlp', ('seq', 'tp')), may hold values from -0.125 to 0.125
- up_weight: bfloat16 [2048, 8192], P('mlp', ('seq', 'tp')), may hold values from -0.125 to 0.125
- down_weight: bfloat16 [8192, 2048], P(('seq', 'tp'), 'mlp'), may hold values from -0.0625 to 0.0625
Outputs:
- updated_hidden: bfloat16 [64, 2048], P('mlp')
- new_keys: bfloat16 [64, 512], P('mlp', 'tp')
- new_values: bfloat16 [64, 512], P('mlp', 'tp')
Inputs may be any that keep to these rules, and one draw needn't show every extreme that they name: `lengths`: one request in every draw has exactly 8192 cached tokens.
All inputs are finite; a program needn't handle non-finite values.
Results may differ from a plain program's by a relative error of at most 0.012.
Values may be sent and summed in bfloat16 or wider, within the bound.
No kernel may reach another device: no remote copies, remote signals or barrier semaphores. Data moves between devices by JAX's collectives and lax.ppermute only.
A program may use at most 64 MiB of HBM per device.

v0:
```python
import jax
import jax.numpy as jnp
from jax import lax
from jax.sharding import PartitionSpec as P

HD = 64


def rms_norm(vectors, weights):
    mean_square = jnp.mean(vectors * vectors, axis=-1, keepdims=True)
    return vectors * lax.rsqrt(mean_square + 1e-05) * weights.astype(jnp.float32)


def rotate(vectors, positions):
    half_dim = vectors.shape[-1] // 2
    inverse = 500000.0 ** (-(jnp.arange(half_dim, dtype=jnp.float32) * 2.0 / vectors.shape[-1]))
    angles = positions.astype(jnp.float32)[:, None] * inverse[None, :]
    cosine = jnp.cos(angles)[:, None, :]
    sine_part = jnp.sin(angles)[:, None, :]
    first_half = vectors[..., :half_dim]
    second_half = vectors[..., half_dim:]
    return jnp.concatenate(
        [
            first_half * cosine - second_half * sine_part,
            second_half * cosine + first_half * sine_part,
        ],
        axis=-1,
    )


def gathered_sum(x, axis):
    return jnp.sum(lax.all_gather(x, axis), axis=0)


def gather_blocks(x, axis):
    size = lax.axis_size(axis)
    me = lax.axis_index(axis)
    held = x[None]
    step = 1
    while step < size:
        other = lax.ppermute(held, axis, [(i, i ^ step) for i in range(size)])
        upper = me // step % 2 == 1
        held = jnp.where(
            upper, jnp.concatenate([other, held], axis=0), jnp.concatenate([held, other], axis=0)
        )
        step *= 2
    return held


def butterfly_sum(x, axis):
    size = lax.axis_size(axis)
    step = 1
    while step < size:
        pairs = [(i, i ^ step) for i in range(size)]
        x = x + lax.ppermute(x, axis, pairs)
        step *= 2
    return x


def per_device(
    hidden,
    lengths,
    attention_gain,
    query_weight,
    key_weight,
    value_weight,
    cached_keys,
    cached_values,
    output_weight,
    feedforward_gain,
    gate_weight,
    up_weight,
    down_weight,
):
    slab_rows, hidden_units = gate_weight.shape
    with jax.named_scope("mlp_weight_gather"):
        slab = jnp.stack(
            [gate_weight, up_weight, down_weight.reshape(slab_rows, hidden_units)], axis=0
        )
        blocks = gather_blocks(slab, "mlp")
    slabs = blocks.shape[0]
    gate_full = blocks[:, 0].reshape(slabs * slab_rows, hidden_units)
    up_full = blocks[:, 1].reshape(slabs * slab_rows, hidden_units)
    down_blocks = blocks[:, 2].reshape(slabs, hidden_units, slab_rows)
    requests = hidden.shape[0]
    stream = hidden.astype(jnp.float32)
    normed = rms_norm(stream, attention_gain).astype(jnp.bfloat16)
    column_width = query_weight.shape[0]
    own_columns = lax.dynamic_slice_in_dim(
        normed, lax.axis_index("seq") * column_width, column_width, 1
    )
    query_width = query_weight.shape[1]
    key_width = key_weight.shape[1]
    with jax.named_scope("qkv_projection"):
        partial = jnp.concatenate(
            [
                jnp.dot(own_columns, query_weight, preferred_element_type=jnp.float32),
                jnp.dot(own_columns, key_weight, preferred_element_type=jnp.float32),
                jnp.dot(own_columns, value_weight, preferred_element_type=jnp.float32),
            ],
            axis=1,
        )
        total = gathered_sum(partial, "seq")
    queries_raw = total[:, :query_width]
    keys_raw = total[:, query_width : query_width + key_width]
    values_raw = total[:, query_width + key_width :]
    local_heads = query_width // HD
    key_heads = key_width // HD
    group_size = local_heads // key_heads
    queries = rotate(queries_raw.reshape(requests, local_heads, HD), lengths).astype(jnp.bfloat16)
    new_keys = (
        rotate(keys_raw.reshape(requests, key_heads, HD), lengths)
        .reshape(requests, key_heads * HD)
        .astype(jnp.bfloat16)
    )
    new_values = values_raw.astype(jnp.bfloat16)
    grouped = queries.reshape(requests, key_heads, group_size, HD)
    block_span = cached_keys.shape[1]
    key_blocks = cached_keys.reshape(requests, block_span, key_heads, HD)
    value_blocks = cached_values.reshape(requests, block_span, key_heads, HD)
    score_scale = HD ** (-0.5)
    first_position = lax.axis_index("seq") * block_span
    positions = first_position + jnp.arange(block_span, dtype=jnp.int32)
    valid_mask = (positions[None, :] < lengths[:, None])[:, None, None, :]
    with jax.named_scope("local_attention"):
        scores = (
            jnp.einsum("rgqd,rpgd->rgqp", grouped, key_blocks, preferred_element_type=jnp.float32)
            * score_scale
        )
        block_max = jnp.max(jnp.where(valid_mask, scores, -1e30), axis=-1)
        exp_weights = jnp.where(valid_mask, jnp.exp(scores - block_max[..., None]), 0.0)
        block_sum = jnp.sum(exp_weights, axis=-1)
        block_acc = jnp.einsum(
            "rgqp,rpgd->rgqd",
            exp_weights.astype(jnp.bfloat16),
            value_blocks,
            preferred_element_type=jnp.float32,
        )
    with jax.named_scope("softmax_merge"):
        state = jnp.concatenate([block_max[..., None], block_sum[..., None], block_acc], axis=-1)
        every_state = lax.all_gather(state, "seq")
        every_max = every_state[..., 0]
        every_sum = every_state[..., 1]
        every_acc = every_state[..., 2:]
        query_float = grouped.astype(jnp.float32)
        self_score = (
            jnp.sum(
                query_float * new_keys.astype(jnp.float32).reshape(requests, key_heads, 1, HD),
                axis=-1,
            )
            * score_scale
        )
        overall_max = jnp.maximum(jnp.max(every_max, axis=0), self_score)
        rescale = jnp.exp(every_max - overall_max[None])
        self_weight = jnp.exp(self_score - overall_max)
        total_weight = jnp.sum(every_sum * rescale, axis=0) + self_weight
        weighted_sum = jnp.sum(every_acc * rescale[..., None], axis=0) + self_weight[
            ..., None
        ] * new_values.astype(jnp.float32).reshape(requests, key_heads, 1, HD)
        attended = (
            (weighted_sum / total_weight[..., None])
            .reshape(requests, local_heads * HD)
            .astype(jnp.bfloat16)
        )
    with jax.named_scope("output_projection"):
        partial_output = jnp.dot(attended, output_weight, preferred_element_type=jnp.float32)
        projected = lax.psum(partial_output, "tp").astype(jnp.bfloat16)
        projected = lax.all_gather(projected, "seq", axis=1, tiled=True)
    mixed_stream = stream + projected.astype(jnp.float32)
    mlp_input = rms_norm(mixed_stream, feedforward_gain).astype(jnp.bfloat16)
    with jax.named_scope("feed_forward"):
        gate = jnp.dot(mlp_input, gate_full, preferred_element_type=jnp.float32)
        upward = jnp.dot(mlp_input, up_full, preferred_element_type=jnp.float32)
        activated = (jax.nn.silu(gate) * upward).astype(jnp.bfloat16)
        down_part = jnp.einsum(
            "rh,jhc->rjc", activated, down_blocks, preferred_element_type=jnp.float32
        ).reshape(requests, slabs * slab_rows)
    with jax.named_scope("down_reduction"):
        down_total = butterfly_sum(gathered_sum(down_part, "tp"), "seq").astype(jnp.bfloat16)
    updated_hidden = (mixed_stream + down_total.astype(jnp.float32)).astype(jnp.bfloat16)
    return (updated_hidden, new_keys, new_values)


def solution(mesh):
    return jax.shard_map(
        per_device,
        mesh=mesh,
        in_specs=(
            P("mlp", None),
            P("mlp"),
            P(),
            P("seq", "tp"),
            P("seq", "tp"),
            P("seq", "tp"),
            P("mlp", "seq", "tp"),
            P("mlp", "seq", "tp"),
            P("tp", "seq"),
            P(),
            P("mlp", ("seq", "tp")),
            P("mlp", ("seq", "tp")),
            P(("seq", "tp"), "mlp"),
        ),
        out_specs=(P("mlp", None), P("mlp", "tp"), P("mlp", "tp")),
        check_vma=False,
    )
```

profile of v0, /device:TPU:64, one launch (start us, length us, event | category | flops | bytes accessed | tf_op | source)
XLA Modules:
  0.0 163.4 jit_solution(15652032731097320502)
XLA Ops:
  0.7 1.0 reshape.177
  1.6 0.9 maximum_bitcast_fusion
  2.5 3.5 %collective-permute-start = (bf16[1,3,256,128]{3,2,1,0:T(8,128)(2,1)S(1)}, bf16[1,3,256,128]{3,2,1,0:T(8,128)(2,1)}, u32[]{:S(2)}, u32[]{:S(2)}) collective-permute-start(bf16[1,3,256,128]{3,2,1,0:T(8,128)(2,1)S(1)} %maximum_bitcast_fusion), channel_id=1, source_target_pairs={{0,4},{4,0},{8,12},{12,8},{16,20},{20,16},{24,28},{28,24},{1,5},{5... | collective-permute-start | bytes 589832 | tf_op jit(solution)/shard_map/mlp_weight_gather/ppermute | solution.py:41
  6.0 0.8 convert_element_type.70
  6.8 0.9 multiply_reduce_fusion.1
  7.7 0.8 dynamic-slice
  8.5 0.2 fusion.26
  8.7 0.9 fusion.24
  9.6 1.0 fusion.28
  10.6 21.2 %all-gather = f32[128,768]{1,0:T(8,128)S(1)} all-gather(f32[8,768]{1,0:T(8,128)S(1)} %pad_maximum_fusion.1), channel_id=2, replica_groups=mesh['seq'=16,'mlp'=8,'tp'=4] {'seq'}, dimensions={0}, use_global_device_ids=true | all-gather | bytes 417792 | tf_op jit(solution)/shard_map/qkv_projection/all_gather | solution.py:32
  32.0 0.5 copy.107
  32.6 0.5 copy.110
  33.3 0.4 select_reduce_fusion
  33.7 0.2 fusion.2
  34.0 0.4 fusion.3
  34.4 0.2 copy.112
  34.6 0.2 copy.111
  34.9 18.2 %all-gather.1 = f32[128,2,4,66]{3,2,1,0:T(4,128)S(1)} all-gather(f32[8,2,4,66]{3,2,1,0:T(4,128)S(1)} %pad_maximum_fusion), channel_id=3, replica_groups=mesh['seq'=16,'mlp'=8,'tp'=4] {'seq'}, dimensions={0}, use_global_device_ids=true | all-gather | bytes 287232 | tf_op jit(solution)/shard_map/softmax_merge/all_gather | solution.py:141
  53.3 0.3 fusion.23
  53.5 0.3 slice-done
  54.1 0.2 multiply_reduce_fusion.2
  54.4 0.5 copy.119
  54.8 0.5 copy.127
  55.4 1.1 maximum_select_fusion.2
  56.6 4.5 %collective-permute-start.1 = (bf16[2,3,256,128]{3,2,1,0:T(8,128)(2,1)S(1)}, bf16[2,3,256,128]{3,2,1,0:T(8,128)(2,1)S(1)}, u32[]{:S(2)}, u32[]{:S(2)}) collective-permute-start(bf16[2,3,256,128]{3,2,1,0:T(8,128)(2,1)S(1)} %maximum_select_fusion.2), channel_id=1, source_target_pairs={{0,8},{4,12},{8,0},{12,4},{16,24},{20,28},{24,16},{28,20},{1,9},{5... | collective-permute-start | bytes 1179656 | tf_op jit(solution)/shard_map/mlp_weight_gather/ppermute | solution.py:41
  61.1 0.2 fusion.10
  61.5 0.3 fusion
  61.8 17.2 %collective-permute-done.1 = bf16[2,3,256,128]{3,2,1,0:T(8,128)(2,1)S(1)} collective-permute-done((bf16[2,3,256,128]{3,2,1,0:T(8,128)(2,1)S(1)}, bf16[2,3,256,128]{3,2,1,0:T(8,128)(2,1)S(1)}, u32[]{:S(2)}, u32[]{:S(2)}) %collective-permute-start.1) | collective-permute-done | bytes 393248 | tf_op jit(solution)/shard_map/mlp_weight_gather/ppermute | solution.py:41
  79.2 6.9 %collective-permute-start.2 = (bf16[4,3,256,128]{3,2,1,0:T(8,128)(2,1)S(1)}, bf16[4,3,256,128]{3,2,1,0:T(8,128)(2,1)S(1)}, u32[]{:S(2)}, u32[]{:S(2)}) collective-permute-start(bf16[4,3,256,128]{3,2,1,0:T(8,128)(2,1)S(1)} %maximum_select_fusion.1), channel_id=1, source_target_pairs={{0,16},{4,20},{8,24},{12,28},{16,0},{20,4},{24,8},{28,12},{1,17},{... | collective-permute-start | bytes 2359304 | tf_op jit(solution)/shard_map/mlp_weight_gather/ppermute | solution.py:41
  86.5 10.5 %psum.7 = bf16[8,128]{1,0:T(8,128)(2,1)S(1)} all-reduce(f32[8,128]{1,0:T(8,128)S(1)} %fusion.30), channel_id=1, replica_groups=mesh['seq'=16,'mlp'=8,'tp'=4] {'tp'}, use_global_device_ids=true, to_apply=%region_8.9 | all-reduce | flops 1024 | bytes 6144 | tf_op jit(solution)/shard_map/output_projection/psum | solution.py:167
  96.9 14.5 %all_gather.22 = bf16[8,2048]{1,0:T(8,128)(2,1)S(1)} all-gather(bf16[8,128]{1,0:T(8,128)(2,1)S(1)} %psum.7), channel_id=1, replica_groups=mesh['seq'=16,'mlp'=8,'tp'=4] {'seq'}, dimensions={1}, use_global_device_ids=true | all-gather | bytes 34816 | tf_op jit(solution)/shard_map/output_projection/all_gather | solution.py:168
  111.6 9.9 %collective-permute-done.2 = bf16[4,3,256,128]{3,2,1,0:T(8,128)(2,1)S(1)} collective-permute-done((bf16[4,3,256,128]{3,2,1,0:T(8,128)(2,1)S(1)}, bf16[4,3,256,128]{3,2,1,0:T(8,128)(2,1)S(1)}, u32[]{:S(2)}, u32[]{:S(2)}) %collective-permute-start.2) | collective-permute-done | bytes 786464 | tf_op jit(solution)/shard_map/mlp_weight_gather/ppermute | solution.py:41
  121.5 0.2 maximum_select_fusion
  121.9 0.2 reshape_squeeze.11
  122.0 0.3 copy.121
  122.3 0.2 fusion.19
  122.6 0.4 fusion.13
  123.0 12.6 %all-gather.2 = f32[32,2048]{1,0:T(8,128)S(1)} all-gather(f32[8,2048]{1,0:T(8,128)S(1)} %fusion.13), channel_id=4, replica_groups=mesh['seq'=16,'mlp'=8,'tp'=4] {'tp'}, dimensions={0}, use_global_device_ids=true | all-gather | bytes 327680 | tf_op jit(solution)/shard_map/down_reduction/all_gather | solution.py:32
  135.6 1.9 %collective-permute-start.3 = (f32[8,2048]{1,0:T(8,128)S(1)}, f32[8,2048]{1,0:T(8,128)S(1)}, u32[]{:S(2)}, u32[]{:S(2)}) collective-permute-start(f32[8,2048]{1,0:T(8,128)S(1)} %bitcast_reduce_fusion.1), channel_id=1, source_target_pairs={{0,32},{32,0},{64,96},{96,64},{128,160},{160,128},{192,224},{224,1... | collective-permute-start | bytes 196616 | tf_op jit(solution)/shard_map/down_reduction/ppermute | solution.py:55
  137.6 1.2 collective-permute-done.3
  138.8 2.3 %collective-permute-start.4 = (f32[8,2048]{1,0:T(8,128)S(1)}, f32[8,2048]{1,0:T(8,128)S(1)}, u32[]{:S(2)}, u32[]{:S(2)}) collective-permute-start(f32[8,2048]{1,0:T(8,128)S(1)} %add.98), channel_id=1, source_target_pairs={{0,64},{32,96},{64,0},{96,32},{128,192},{160,224},{192,128},{224,1... | collective-permute-start | bytes 196616 | tf_op jit(solution)/shard_map/down_reduction/ppermute | solution.py:55
  141.1 3.9 %collective-permute-done.4 = f32[8,2048]{1,0:T(8,128)S(1)} collective-permute-done((f32[8,2048]{1,0:T(8,128)S(1)}, f32[8,2048]{1,0:T(8,128)S(1)}, u32[]{:S(2)}, u32[]{:S(2)}) %collective-permute-start.4) | collective-permute-done | bytes 65568 | tf_op jit(solution)/shard_map/down_reduction/ppermute | solution.py:55
  145.0 2.2 %collective-permute-start.5 = (f32[8,2048]{1,0:T(8,128)S(1)}, f32[8,2048]{1,0:T(8,128)S(1)}, u32[]{:S(2)}, u32[]{:S(2)}) collective-permute-start(f32[8,2048]{1,0:T(8,128)S(1)} %add.99), channel_id=1, source_target_pairs={{0,128},{32,160},{64,192},{96,224},{128,0},{160,32},{192,64},{224,... | collective-permute-start | bytes 196616 | tf_op jit(solution)/shard_map/down_reduction/ppermute | solution.py:55
  147.1 4.9 %collective-permute-done.5 = f32[8,2048]{1,0:T(8,128)S(1)} collective-permute-done((f32[8,2048]{1,0:T(8,128)S(1)}, f32[8,2048]{1,0:T(8,128)S(1)}, u32[]{:S(2)}, u32[]{:S(2)}) %collective-permute-start.5) | collective-permute-done | bytes 65568 | tf_op jit(solution)/shard_map/down_reduction/ppermute | solution.py:55
  152.0 3.4 %collective-permute-start.6 = (f32[8,2048]{1,0:T(8,128)S(1)}, f32[8,2048]{1,0:T(8,128)S(1)}, u32[]{:S(2)}, u32[]{:S(2)}) collective-permute-start(f32[8,2048]{1,0:T(8,128)S(1)} %add.100), channel_id=1, source_target_pairs={{0,256},{32,288},{64,320},{96,352},{128,384},{160,416},{192,448},{... | collective-permute-start | bytes 196616 | tf_op jit(solution)/shard_map/down_reduction/ppermute | solution.py:55
  155.4 0.7 convert_element_type.88
  156.1 6.7 %collective-permute-done.6 = f32[8,2048]{1,0:T(8,128)S(1)} collective-permute-done((f32[8,2048]{1,0:T(8,128)S(1)}, f32[8,2048]{1,0:T(8,128)S(1)}, u32[]{:S(2)}, u32[]{:S(2)}) %collective-permute-start.6) | collective-permute-done | bytes 65568 | tf_op jit(solution)/shard_map/down_reduction/ppermute | solution.py:55
  162.8 0.6 add_convert_fusion
  (59 shorter events, 2.0 us)
Async XLA Ops:
  0.6 7.8 %copy-start = (bf16[128,512]{1,0:T(8,128)(2,1)S(1)}, bf16[128,512]{1,0:T(8,128)(2,1)}, u32[]{:S(2)}) copy-start(bf16[128,512]{1,0:T(8,128)(2,1)} %param.16) | copy-start | bytes 393220
  0.6 31.3 %copy-start.9 = (s32[8]{0:T(128)S(1)}, s32[8]{0:T(128)}, u32[]{:S(2)}) copy-start(s32[8]{0:T(128)} %param.14) | copy-start | bytes 100
  0.7 31.4 %copy-start.2 = (bf16[8,512,128]{2,1,0:T(8,128)(2,1)S(1)}, bf16[8,512,128]{2,1,0:T(8,128)(2,1)}, u32[]{:S(2)}) copy-start(bf16[8,512,128]{2,1,0:T(8,128)(2,1)} %param.19) | copy-start | bytes 3145732
  2.5 52.9 %collective-permute-start = (bf16[1,3,256,128]{3,2,1,0:T(8,128)(2,1)S(1)}, bf16[1,3,256,128]{3,2,1,0:T(8,128)(2,1)}, u32[]{:S(2)}, u32[]{:S(2)}) collective-permute-start(bf16[1,3,256,128]{3,2,1,0:T(8,128)(2,1)S(1)} %maximum_bitcast_fusion), channel_id=1, source_target_pairs={{0,4},{4,0},{8,12},{12,8},{16,20},{20,16},{24,28},{28,24},{1,5},{5... | collective-permute-start | bytes 589832 | tf_op jit(solution)/shard_map/mlp_weight_gather/ppermute | solution.py:41
  9.6 23.0 %copy-start.3 = (bf16[8,512,128]{2,1,0:T(8,128)(2,1)S(1)}, bf16[8,512,128]{2,1,0:T(8,128)(2,1)}, u32[]{:S(2)}) copy-start(bf16[8,512,128]{2,1,0:T(8,128)(2,1)} %param.20) | copy-start | bytes 3145732
  31.8 1.3 copy-start.5
  53.2 0.7 slice-start
  53.8 7.4 %copy-start.6 = (f32[8,768]{1,0:T(8,128)S(1)}, f32[8,768]{1,0:T(8,128)}, u32[]{:S(2)}) copy-start(f32[8,768]{1,0:T(8,128)} %copy-done.5) | copy-start | bytes 73732
  55.4 30.9 %copy-start.8 = (bf16[2048]{0:T(1024)(128)(2,1)S(1)}, bf16[2048]{0:T(1024)(128)(2,1)}, u32[]{:S(2)}) copy-start(bf16[2048]{0:T(1024)(128)(2,1)} %param.22) | copy-start | bytes 12292
  55.4 30.9 %copy-start.4 = (bf16[512,128]{1,0:T(8,128)(2,1)S(1)}, bf16[512,128]{1,0:T(8,128)(2,1)}, u32[]{:S(2)}) copy-start(bf16[512,128]{1,0:T(8,128)(2,1)} %param.21) | copy-start | bytes 393220
  56.5 54.9 %copy-start.1 = (bf16[8,2048]{1,0:T(8,128)(2,1)S(1)}, bf16[8,2048]{1,0:T(8,128)(2,1)}, u32[]{:S(2)}) copy-start(bf16[8,2048]{1,0:T(8,128)(2,1)} %param.13) | copy-start | bytes 98308
  56.6 22.5 %collective-permute-start.1 = (bf16[2,3,256,128]{3,2,1,0:T(8,128)(2,1)S(1)}, bf16[2,3,256,128]{3,2,1,0:T(8,128)(2,1)S(1)}, u32[]{:S(2)}, u32[]{:S(2)}) collective-permute-start(bf16[2,3,256,128]{3,2,1,0:T(8,128)(2,1)S(1)} %maximum_select_fusion.2), channel_id=1, source_target_pairs={{0,8},{4,12},{8,0},{12,4},{16,24},{20,28},{24,16},{28,20},{1,9},{5... | collective-permute-start | bytes 1179656 | tf_op jit(solution)/shard_map/mlp_weight_gather/ppermute | solution.py:41
  61.3 60.5 %copy-start.7 = (bf16[8,128]{1,0:T(8,128)(2,1)}, bf16[8,128]{1,0:T(8,128)(2,1)S(1)}, u32[]{:S(2)}) copy-start(bf16[8,128]{1,0:T(8,128)(2,1)S(1)} %slice.79) | copy-start | bytes 6148
  79.2 42.3 %collective-permute-start.2 = (bf16[4,3,256,128]{3,2,1,0:T(8,128)(2,1)S(1)}, bf16[4,3,256,128]{3,2,1,0:T(8,128)(2,1)S(1)}, u32[]{:S(2)}, u32[]{:S(2)}) collective-permute-start(bf16[4,3,256,128]{3,2,1,0:T(8,128)(2,1)S(1)} %maximum_select_fusion.1), channel_id=1, source_target_pairs={{0,16},{4,20},{8,24},{12,28},{16,0},{20,4},{24,8},{28,12},{1,17},{... | collective-permute-start | bytes 2359304 | tf_op jit(solution)/shard_map/mlp_weight_gather/ppermute | solution.py:41
  135.6 3.1 %collective-permute-start.3 = (f32[8,2048]{1,0:T(8,128)S(1)}, f32[8,2048]{1,0:T(8,128)S(1)}, u32[]{:S(2)}, u32[]{:S(2)}) collective-permute-start(f32[8,2048]{1,0:T(8,128)S(1)} %bitcast_reduce_fusion.1), channel_id=1, source_target_pairs={{0,32},{32,0},{64,96},{96,64},{128,160},{160,128},{192,224},{224,1... | collective-permute-start | bytes 196616 | tf_op jit(solution)/shard_map/down_reduction/ppermute | solution.py:55
  138.8 6.2 %collective-permute-start.4 = (f32[8,2048]{1,0:T(8,128)S(1)}, f32[8,2048]{1,0:T(8,128)S(1)}, u32[]{:S(2)}, u32[]{:S(2)}) collective-permute-start(f32[8,2048]{1,0:T(8,128)S(1)} %add.98), channel_id=1, source_target_pairs={{0,64},{32,96},{64,0},{96,32},{128,192},{160,224},{192,128},{224,1... | collective-permute-start | bytes 196616 | tf_op jit(solution)/shard_map/down_reduction/ppermute | solution.py:55
  145.0 7.1 %collective-permute-start.5 = (f32[8,2048]{1,0:T(8,128)S(1)}, f32[8,2048]{1,0:T(8,128)S(1)}, u32[]{:S(2)}, u32[]{:S(2)}) collective-permute-start(f32[8,2048]{1,0:T(8,128)S(1)} %add.99), channel_id=1, source_target_pairs={{0,128},{32,160},{64,192},{96,224},{128,0},{160,32},{192,64},{224,... | collective-permute-start | bytes 196616 | tf_op jit(solution)/shard_map/down_reduction/ppermute | solution.py:55
  152.0 10.8 %collective-permute-start.6 = (f32[8,2048]{1,0:T(8,128)S(1)}, f32[8,2048]{1,0:T(8,128)S(1)}, u32[]{:S(2)}, u32[]{:S(2)}) collective-permute-start(f32[8,2048]{1,0:T(8,128)S(1)} %add.100), channel_id=1, source_target_pairs={{0,256},{32,288},{64,320},{96,352},{128,384},{160,416},{192,448},{... | collective-permute-start | bytes 196616 | tf_op jit(solution)/shard_map/down_reduction/ppermute | solution.py:55
where the time goes:
time: 164 us; the launch traced here: 163 us
  blocking collectives  77 us (47%)
  waiting for transfers between devices  43.8 us (27%)
  starting transfers between devices  24.6 us (15%)
  other arithmetic  6.82 us (4%)
  local copies, waits for them, and re-layouts  6.29 us (4%)
  matrix products  3.79 us (2%)
    all_gather x2, blocking collectives, gathered_sum(): return jnp.sum(lax.all_gather(x, axis), axis=0)  33.8 us
    ppermute x3, waiting for transfers between devices, gather_blocks(): other = lax.ppermute(held, axis, [(i, i ^ step) for i in range(size)])  27.1 us
    all_gather x1, blocking collectives, per_device(): every_state = lax.all_gather(state, 'seq')  18.2 us
    ppermute x4, waiting for transfers between devices, butterfly_sum(): x = x + lax.ppermute(x, axis, pairs)  16.8 us
    ppermute x3, starting transfers between devices, gather_blocks(): other = lax.ppermute(held, axis, [(i, i ^ step) for i in range(size)])  14.9 us
    all_gather x1, blocking collectives, per_device(): projected = lax.all_gather(projected, 'seq', axis=1, tiled=True)  14.5 us
    psum x1, blocking collectives, per_device(): projected = lax.psum(partial_output, 'tp').astype(jnp.bfloat16)  10.5 us
    ppermute x4, starting transfers between devices, butterfly_sum(): x = x + lax.ppermute(x, axis, pairs)  9.69 us
  transfers between devices with their start and end apart: 7, of which 6 were waited for; matrix products, arithmetic and copies ran while one was open for 7% of the time, Pallas kernels for 0%

commit v1 on v0

--- a/solution.py
+++ b/solution.py
@@ -4,6 +4,11 @@
 from jax.sharding import PartitionSpec as P
 
 HD = 64
+
+
+def tiled_gather(array, axis, dim):
+    copies = jnp.concatenate([array] * lax.axis_size(axis), axis=dim)
+    return lax.all_to_all(copies, axis, dim, dim, tiled=True)
 
 
 def rms_norm(vectors, weights):
@@ -165,7 +170,7 @@
     with jax.named_scope("output_projection"):
         partial_output = jnp.dot(attended, output_weight, preferred_element_type=jnp.float32)
         projected = lax.psum(partial_output, "tp").astype(jnp.bfloat16)
-        projected = lax.all_gather(projected, "seq", axis=1, tiled=True)
+        projected = tiled_gather(projected, "seq", 1)
     mixed_stream = stream + projected.astype(jnp.float32)
     mlp_input = rms_norm(mixed_stream, feedforward_gain).astype(jnp.bfloat16)
     with jax.named_scope("feed_forward"):

time: 164 us -> 178 us (1.085)
  waiting for transfers between devices: 43.8 us -> 59.5 us
  blocking collectives: 77 us -> 62.3 us
  local copies, waits for them, and re-layouts: 6.29 us -> 15.6 us
  starting transfers between devices: 24.6 us -> 28.3 us
    all_gather x1 -> x0, blocking collectives: 14.5 us -> none  [per_device(): projected = lax.all_gather(projected, 'seq', axis=1, tiled=True)]
    ppermute x3, waiting for transfers between devices: 27.1 us -> 36.4 us  [gather_blocks(): other = lax.ppermute(held, axis, [(i, i ^ step) for i in range(size)])]
    unnamed x23 -> x36, local copies, waits for them, and re-layouts: 1.58 us -> 10.3 us
    all_to_all x0 -> x1, waiting for transfers between devices: none -> 6.34 us  [tiled_gather(): return lax.all_to_all(copies, axis, dim, dim, tiled=True)]
    all_to_all x0 -> x1, starting transfers between devices: none -> 3.64 us  [tiled_gather(): return lax.all_to_all(copies, axis, dim, dim, tiled=True)]
  transfers between devices with their start and end apart: 7 -> 8, of which waited for: 6 -> 7; matrix products, arithmetic and copies ran while one was open for 7% -> 12% of each run, Pallas kernels for 0% -> 0%
where the time goes in v1:
time: 178 us; the launch traced here: 177 us
  blocking collectives  62.3 us (35%)
  waiting for transfers between devices  59.5 us (33%)
  starting transfers between devices  28.3 us (16%)
  local copies, waits for them, and re-layouts  15.6 us (9%)
  other arithmetic  6.78 us (4%)
  matrix products  3.7 us (2%)
    ppermute x3, waiting for transfers between devices, gather_blocks(): other = lax.ppermute(held, axis, [(i, i ^ step) for i in range(size)])  36.4 us
    all_gather x2, blocking collectives, gathered_sum(): return jnp.sum(lax.all_gather(x, axis), axis=0)  33.6 us
    all_gather x1, blocking collectives, per_device(): every_state = lax.all_gather(state, 'seq')  18.2 us
    ppermute x4, waiting for transfers between devices, butterfly_sum(): x = x + lax.ppermute(x, axis, pairs)  16.8 us
    ppermute x3, starting transfers between devices, gather_blocks(): other = lax.ppermute(held, axis, [(i, i ^ step) for i in range(size)])  14.9 us
    psum x1, blocking collectives, per_device(): projected = lax.psum(partial_output, 'tp').astype(jnp.bfloat16)  10.5 us
    unnamed x36, local copies, waits for them, and re-layouts  10.3 us
    ppermute x4, starting transfers between devices, butterfly_sum(): x = x + lax.ppermute(x, axis, pairs)  9.69 us
  transfers between devices with their start and end apart: 8, of which 7 were waited for; matrix products, arithmetic and copies ran while one was open for 12% of the time, Pallas kernels for 0%

profile of v1, /device:TPU:64, one launch (start us, length us, event | category | flops | bytes accessed | tf_op | source)
XLA Modules:
  0.0 177.1 jit_solution(13447083995003345248)
XLA Ops:
  0.7 1.0 reshape.181
  1.6 0.9 maximum_bitcast_fusion
  2.5 3.5 %collective-permute-start = (bf16[1,3,256,128]{3,2,1,0:T(8,128)(2,1)S(1)}, bf16[1,3,256,128]{3,2,1,0:T(8,128)(2,1)}, u32[]{:S(2)}, u32[]{:S(2)}) collective-permute-start(bf16[1,3,256,128]{3,2,1,0:T(8,128)(2,1)S(1)} %maximum_bitcast_fusion), channel_id=1, source_target_pairs={{0,4},{4,0},{8,12},{12,8},{16,20},{20,16},{24,28},{28,24},{1,5},{5... | collective-permute-start | bytes 589832 | tf_op jit(solution)/shard_map/mlp_weight_gather/ppermute | solution.py:46
  6.0 0.8 convert_element_type.73
  6.8 0.9 multiply_reduce_fusion.1
  7.7 0.8 dynamic-slice
  8.7 0.9 fusion.24
  9.6 0.9 fusion.28
  10.5 21.3 %all-gather = f32[128,768]{1,0:T(8,128)S(1)} all-gather(f32[8,768]{1,0:T(8,128)S(1)} %pad_maximum_fusion.1), channel_id=2, replica_groups=mesh['seq'=16,'mlp'=8,'tp'=4] {'seq'}, dimensions={0}, use_global_device_ids=true | all-gather | bytes 417792 | tf_op jit(solution)/shard_map/qkv_projection/all_gather | solution.py:37
  32.1 0.5 copy.107
  32.7 0.5 copy.110
  35.0 18.2 %all-gather.1 = f32[128,2,4,66]{3,2,1,0:T(4,128)S(1)} all-gather(f32[8,2,4,66]{3,2,1,0:T(4,128)S(1)} %pad_maximum_fusion), channel_id=3, replica_groups=mesh['seq'=16,'mlp'=8,'tp'=4] {'seq'}, dimensions={0}, use_global_device_ids=true | all-gather | bytes 287232 | tf_op jit(solution)/shard_map/softmax_merge/all_gather | solution.py:146
  54.9 0.5 copy.127
  56.5 10.5 %psum.7 = bf16[8,128]{1,0:T(8,128)(2,1)S(1)} all-reduce(f32[8,128]{1,0:T(8,128)S(1)} %fusion.30), channel_id=1, replica_groups=mesh['seq'=16,'mlp'=8,'tp'=4] {'tp'}, use_global_device_ids=true, to_apply=%region_8.9 | all-reduce | flops 1024 | bytes 6144 | tf_op jit(solution)/shard_map/output_projection/psum | solution.py:172
  67.0 0.6 constant_dynamic-update-slice_fusion.15
  67.6 0.6 constant_dynamic-update-slice_fusion.14
  68.2 0.6 constant_dynamic-update-slice_fusion.13
  68.8 0.6 constant_dynamic-update-slice_fusion.12
  69.3 0.6 constant_dynamic-update-slice_fusion.11
  69.9 0.6 constant_dynamic-update-slice_fusion.10
  70.5 0.6 constant_dynamic-update-slice_fusion.9
  71.1 0.6 constant_dynamic-update-slice_fusion.8
  71.7 1.1 maximum_select_fusion.2
  72.7 4.5 %collective-permute-start.1 = (bf16[2,3,256,128]{3,2,1,0:T(8,128)(2,1)S(1)}, bf16[2,3,256,128]{3,2,1,0:T(8,128)(2,1)S(1)}, u32[]{:S(2)}, u32[]{:S(2)}) collective-permute-start(bf16[2,3,256,128]{3,2,1,0:T(8,128)(2,1)S(1)} %maximum_select_fusion.2), channel_id=1, source_target_pairs={{0,8},{4,12},{8,0},{12,4},{16,24},{20,28},{24,16},{28,20},{1,9},{5... | collective-permute-start | bytes 1179656 | tf_op jit(solution)/shard_map/mlp_weight_gather/ppermute | solution.py:46
  77.2 0.6 constant_dynamic-update-slice_fusion.7
  77.8 0.6 constant_dynamic-update-slice_fusion.6
  78.4 0.6 constant_dynamic-update-slice_fusion.5
  79.0 0.6 constant_dynamic-update-slice_fusion.4
  79.6 13.6 %collective-permute-done.1 = bf16[2,3,256,128]{3,2,1,0:T(8,128)(2,1)S(1)} collective-permute-done((bf16[2,3,256,128]{3,2,1,0:T(8,128)(2,1)S(1)}, bf16[2,3,256,128]{3,2,1,0:T(8,128)(2,1)S(1)}, u32[]{:S(2)}, u32[]{:S(2)}) %collective-permute-start.1) | collective-permute-done | bytes 393248 | tf_op jit(solution)/shard_map/mlp_weight_gather/ppermute | solution.py:46
  93.3 6.9 %collective-permute-start.2 = (bf16[4,3,256,128]{3,2,1,0:T(8,128)(2,1)S(1)}, bf16[4,3,256,128]{3,2,1,0:T(8,128)(2,1)S(1)}, u32[]{:S(2)}, u32[]{:S(2)}) collective-permute-start(bf16[4,3,256,128]{3,2,1,0:T(8,128)(2,1)S(1)} %maximum_select_fusion.1), channel_id=1, source_target_pairs={{0,16},{4,20},{8,24},{12,28},{16,0},{20,4},{24,8},{28,12},{1,17},{... | collective-permute-start | bytes 2359304 | tf_op jit(solution)/shard_map/mlp_weight_gather/ppermute | solution.py:46
  100.3 0.6 constant_dynamic-update-slice_fusion.3
  100.9 0.6 constant_dynamic-update-slice_fusion.2
  101.4 0.6 constant_dynamic-update-slice_fusion.1
  102.0 0.6 constant_dynamic-update-slice_fusion
  102.6 3.6 %all-to-all-start = ((bf16[8,16,128]{2,0,1:T(8,128)(2,1)}), bf16[8,16,128]{2,0,1:T(8,128)(2,1)S(1)}, u32[]{:S(2)}, u32[]{:S(2)}) async-start(bf16[8,16,128]{2,0,1:T(8,128)(2,1)} %bitcast.11), calls=%async_computation | async-start | bytes 65536 | tf_op jit(solution)/shard_map/output_projection/all_to_all | solution.py:11
  106.3 6.3 %all-to-all-done = bf16[8,16,128]{2,0,1:T(8,128)(2,1)S(1)} async-done(((bf16[8,16,128]{2,0,1:T(8,128)(2,1)}), bf16[8,16,128]{2,0,1:T(8,128)(2,1)S(1)}, u32[]{:S(2)}, u32[]{:S(2)}) %all-to-all-start) | async-done | bytes 32800 | tf_op jit(solution)/shard_map/output_projection/all_to_all | solution.py:11
  112.7 22.8 %collective-permute-done.2 = bf16[4,3,256,128]{3,2,1,0:T(8,128)(2,1)S(1)} collective-permute-done((bf16[4,3,256,128]{3,2,1,0:T(8,128)(2,1)S(1)}, bf16[4,3,256,128]{3,2,1,0:T(8,128)(2,1)S(1)}, u32[]{:S(2)}, u32[]{:S(2)}) %collective-permute-start.2) | collective-permute-done | bytes 786464 | tf_op jit(solution)/shard_map/mlp_weight_gather/ppermute | solution.py:46
  137.0 12.3 %all-gather.2 = f32[32,2048]{1,0:T(8,128)S(1)} all-gather(f32[8,2048]{1,0:T(8,128)S(1)} %fusion.13), channel_id=4, replica_groups=mesh['seq'=16,'mlp'=8,'tp'=4] {'tp'}, dimensions={0}, use_global_device_ids=true | all-gather | bytes 327680 | tf_op jit(solution)/shard_map/down_reduction/all_gather | solution.py:37
  149.3 1.9 %collective-permute-start.3 = (f32[8,2048]{1,0:T(8,128)S(1)}, f32[8,2048]{1,0:T(8,128)S(1)}, u32[]{:S(2)}, u32[]{:S(2)}) collective-permute-start(f32[8,2048]{1,0:T(8,128)S(1)} %bitcast_reduce_fusion.1), channel_id=1, source_target_pairs={{0,32},{32,0},{64,96},{96,64},{128,160},{160,128},{192,224},{224,1... | collective-permute-start | bytes 196616 | tf_op jit(solution)/shard_map/down_reduction/ppermute | solution.py:60
  151.2 1.2 collective-permute-done.3
  152.4 2.3 %collective-permute-start.4 = (f32[8,2048]{1,0:T(8,128)S(1)}, f32[8,2048]{1,0:T(8,128)S(1)}, u32[]{:S(2)}, u32[]{:S(2)}) collective-permute-start(f32[8,2048]{1,0:T(8,128)S(1)} %add.98), channel_id=1, source_target_pairs={{0,64},{32,96},{64,0},{96,32},{128,192},{160,224},{192,128},{224,1... | collective-permute-start | bytes 196616 | tf_op jit(solution)/shard_map/down_reduction/ppermute | solution.py:60
  154.7 3.9 %collective-permute-done.4 = f32[8,2048]{1,0:T(8,128)S(1)} collective-permute-done((f32[8,2048]{1,0:T(8,128)S(1)}, f32[8,2048]{1,0:T(8,128)S(1)}, u32[]{:S(2)}, u32[]{:S(2)}) %collective-permute-start.4) | collective-permute-done | bytes 65568 | tf_op jit(solution)/shard_map/down_reduction/ppermute | solution.py:60
  158.6 2.2 %collective-permute-start.5 = (f32[8,2048]{1,0:T(8,128)S(1)}, f32[8,2048]{1,0:T(8,128)S(1)}, u32[]{:S(2)}, u32[]{:S(2)}) collective-permute-start(f32[8,2048]{1,0:T(8,128)S(1)} %add.99), channel_id=1, source_target_pairs={{0,128},{32,160},{64,192},{96,224},{128,0},{160,32},{192,64},{224,... | collective-permute-start | bytes 196616 | tf_op jit(solution)/shard_map/down_reduction/ppermute | solution.py:60
  160.8 4.9 %collective-permute-done.5 = f32[8,2048]{1,0:T(8,128)S(1)} collective-permute-done((f32[8,2048]{1,0:T(8,128)S(1)}, f32[8,2048]{1,0:T(8,128)S(1)}, u32[]{:S(2)}, u32[]{:S(2)}) %collective-permute-start.5) | collective-permute-done | bytes 65568 | tf_op jit(solution)/shard_map/down_reduction/ppermute | solution.py:60
  165.7 3.4 %collective-permute-start.6 = (f32[8,2048]{1,0:T(8,128)S(1)}, f32[8,2048]{1,0:T(8,128)S(1)}, u32[]{:S(2)}, u32[]{:S(2)}) collective-permute-start(f32[8,2048]{1,0:T(8,128)S(1)} %add.100), channel_id=1, source_target_pairs={{0,256},{32,288},{64,320},{96,352},{128,384},{160,416},{192,448},{... | collective-permute-start | bytes 196616 | tf_op jit(solution)/shard_map/down_reduction/ppermute | solution.py:60
  169.0 0.7 convert_element_type.92
  169.7 6.7 %collective-permute-done.6 = f32[8,2048]{1,0:T(8,128)S(1)} collective-permute-done((f32[8,2048]{1,0:T(8,128)S(1)}, f32[8,2048]{1,0:T(8,128)S(1)}, u32[]{:S(2)}, u32[]{:S(2)}) %collective-permute-start.6) | collective-permute-done | bytes 65568 | tf_op jit(solution)/shard_map/down_reduction/ppermute | solution.py:60
  176.5 0.6 add_convert_fusion
  (74 shorter events, 6.7 us)
Async XLA Ops:
  0.6 7.8 %copy-start = (bf16[128,512]{1,0:T(8,128)(2,1)S(1)}, bf16[128,512]{1,0:T(8,128)(2,1)}, u32[]{:S(2)}) copy-start(bf16[128,512]{1,0:T(8,128)(2,1)} %param.16) | copy-start | bytes 393220
  0.6 31.4 %copy-start.8 = (s32[8]{0:T(128)S(1)}, s32[8]{0:T(128)}, u32[]{:S(2)}) copy-start(s32[8]{0:T(128)} %param.14) | copy-start | bytes 100
  0.7 31.5 %copy-start.2 = (bf16[8,512,128]{2,1,0:T(8,128)(2,1)S(1)}, bf16[8,512,128]{2,1,0:T(8,128)(2,1)}, u32[]{:S(2)}) copy-start(bf16[8,512,128]{2,1,0:T(8,128)(2,1)} %param.19) | copy-start | bytes 3145732
  2.5 69.1 %collective-permute-start = (bf16[1,3,256,128]{3,2,1,0:T(8,128)(2,1)S(1)}, bf16[1,3,256,128]{3,2,1,0:T(8,128)(2,1)}, u32[]{:S(2)}, u32[]{:S(2)}) collective-permute-start(bf16[1,3,256,128]{3,2,1,0:T(8,128)(2,1)S(1)} %maximum_bitcast_fusion), channel_id=1, source_target_pairs={{0,4},{4,0},{8,12},{12,8},{16,20},{20,16},{24,28},{28,24},{1,5},{5... | collective-permute-start | bytes 589832 | tf_op jit(solution)/shard_map/mlp_weight_gather/ppermute | solution.py:46
  10.5 22.1 %copy-start.3 = (bf16[8,512,128]{2,1,0:T(8,128)(2,1)S(1)}, bf16[8,512,128]{2,1,0:T(8,128)(2,1)}, u32[]{:S(2)}) copy-start(bf16[8,512,128]{2,1,0:T(8,128)(2,1)} %param.20) | copy-start | bytes 3145732
  31.9 1.3 copy-start.5
  31.9 24.2 %copy-start.6 = (bf16[8,128]{1,0:T(8,128)(2,1)}, bf16[8,128]{1,0:T(8,128)(2,1)S(1)}, u32[]{:S(2)}) copy-start(bf16[8,128]{1,0:T(8,128)(2,1)S(1)} %slice.79) | copy-start | bytes 6148
  53.2 0.7 slice-start
  53.9 2.5 %copy-start.4 = (bf16[512,128]{1,0:T(8,128)(2,1)S(1)}, bf16[512,128]{1,0:T(8,128)(2,1)}, u32[]{:S(2)}) copy-start(bf16[512,128]{1,0:T(8,128)(2,1)} %param.21) | copy-start | bytes 393220
  56.1 50.1 %copy-start.7 = (bf16[2048]{0:T(1024)(128)(2,1)S(1)}, bf16[2048]{0:T(1024)(128)(2,1)}, u32[]{:S(2)}) copy-start(bf16[2048]{0:T(1024)(128)(2,1)} %param.22) | copy-start | bytes 12292
  56.1 56.5 %copy-start.1 = (bf16[8,2048]{1,0:T(8,128)(2,1)S(1)}, bf16[8,2048]{1,0:T(8,128)(2,1)}, u32[]{:S(2)}) copy-start(bf16[8,2048]{1,0:T(8,128)(2,1)} %param.13) | copy-start | bytes 98308
  72.7 20.5 %collective-permute-start.1 = (bf16[2,3,256,128]{3,2,1,0:T(8,128)(2,1)S(1)}, bf16[2,3,256,128]{3,2,1,0:T(8,128)(2,1)S(1)}, u32[]{:S(2)}, u32[]{:S(2)}) collective-permute-start(bf16[2,3,256,128]{3,2,1,0:T(8,128)(2,1)S(1)} %maximum_select_fusion.2), channel_id=1, source_target_pairs={{0,8},{4,12},{8,0},{12,4},{16,24},{20,28},{24,16},{28,20},{1,9},{5... | collective-permute-start | bytes 1179656 | tf_op jit(solution)/shard_map/mlp_weight_gather/ppermute | solution.py:46
  93.3 42.2 %collective-permute-start.2 = (bf16[4,3,256,128]{3,2,1,0:T(8,128)(2,1)S(1)}, bf16[4,3,256,128]{3,2,1,0:T(8,128)(2,1)S(1)}, u32[]{:S(2)}, u32[]{:S(2)}) collective-permute-start(bf16[4,3,256,128]{3,2,1,0:T(8,128)(2,1)S(1)} %maximum_select_fusion.1), channel_id=1, source_target_pairs={{0,16},{4,20},{8,24},{12,28},{16,0},{20,4},{24,8},{28,12},{1,17},{... | collective-permute-start | bytes 2359304 | tf_op jit(solution)/shard_map/mlp_weight_gather/ppermute | solution.py:46
  102.6 10.0 %all-to-all-start = ((bf16[8,16,128]{2,0,1:T(8,128)(2,1)}), bf16[8,16,128]{2,0,1:T(8,128)(2,1)S(1)}, u32[]{:S(2)}, u32[]{:S(2)}) async-start(bf16[8,16,128]{2,0,1:T(8,128)(2,1)} %bitcast.11), calls=%async_computation | async-start | bytes 65536 | tf_op jit(solution)/shard_map/output_projection/all_to_all | solution.py:11
  149.3 3.1 %collective-permute-start.3 = (f32[8,2048]{1,0:T(8,128)S(1)}, f32[8,2048]{1,0:T(8,128)S(1)}, u32[]{:S(2)}, u32[]{:S(2)}) collective-permute-start(f32[8,2048]{1,0:T(8,128)S(1)} %bitcast_reduce_fusion.1), channel_id=1, source_target_pairs={{0,32},{32,0},{64,96},{96,64},{128,160},{160,128},{192,224},{224,1... | collective-permute-start | bytes 196616 | tf_op jit(solution)/shard_map/down_reduction/ppermute | solution.py:60
  152.4 6.2 %collective-permute-start.4 = (f32[8,2048]{1,0:T(8,128)S(1)}, f32[8,2048]{1,0:T(8,128)S(1)}, u32[]{:S(2)}, u32[]{:S(2)}) collective-permute-start(f32[8,2048]{1,0:T(8,128)S(1)} %add.98), channel_id=1, source_target_pairs={{0,64},{32,96},{64,0},{96,32},{128,192},{160,224},{192,128},{224,1... | collective-permute-start | bytes 196616 | tf_op jit(solution)/shard_map/down_reduction/ppermute | solution.py:60
  158.6 7.1 %collective-permute-start.5 = (f32[8,2048]{1,0:T(8,128)S(1)}, f32[8,2048]{1,0:T(8,128)S(1)}, u32[]{:S(2)}, u32[]{:S(2)}) collective-permute-start(f32[8,2048]{1,0:T(8,128)S(1)} %add.99), channel_id=1, source_target_pairs={{0,128},{32,160},{64,192},{96,224},{128,0},{160,32},{192,64},{224,... | collective-permute-start | bytes 196616 | tf_op jit(solution)/shard_map/down_reduction/ppermute | solution.py:60
  165.7 10.8 %collective-permute-start.6 = (f32[8,2048]{1,0:T(8,128)S(1)}, f32[8,2048]{1,0:T(8,128)S(1)}, u32[]{:S(2)}, u32[]{:S(2)}) collective-permute-start(f32[8,2048]{1,0:T(8,128)S(1)} %add.100), channel_id=1, source_target_pairs={{0,256},{32,288},{64,320},{96,352},{128,384},{160,416},{192,448},{... | collective-permute-start | bytes 196616 | tf_op jit(solution)/shard_map/down_reduction/ppermute | solution.py:60
